TPU v7x, 256 devices: a whole 4x4x8 slice. The times are simulated.
256 devices in a mesh: grp: 4 (over y), mdl: 64 (over z, x, core).
Axes of the slice: x: 4, y: 4, z: 8, core: 2. Of those that a mesh axis runs over, the one named last changes fastest.
Arguments:
- pol_hidden: bfloat16 [1024, 4096], P(('grp', 'mdl')), may hold values from -6 to 6
- ref_hidden: bfloat16 [1024, 4096], P(('grp', 'mdl')), may hold values from -6 to 6
- pol_mlp_gain: bfloat16 [4096], replicated, may hold values from 0.099609375 to 1.8984375
- ref_mlp_gain: bfloat16 [4096], replicated, may hold values from 0.099609375 to 1.8984375
- pol_final_gain: bfloat16 [4096], replicated, may hold values from 0.099609375 to 1.8984375
- ref_final_gain: bfloat16 [4096], replicated, may hold values from 0.099609375 to 1.8984375
- pol_gate: bfloat16 [4096, 11008], P(None, 'mdl'), may hold values from -0.09375 to 0.09375
- pol_up: bfloat16 [4096, 11008], P(None, 'mdl'), may hold values from -0.09375 to 0.09375
- pol_down: bfloat16 [11008, 4096], P('mdl'), may hold values from -0.109375 to 0.109375
- ref_gate: bfloat16 [4096, 11008], P(None, 'mdl'), may hold values from -0.09375 to 0.09375
- ref_up: bfloat16 [4096, 11008], P(None, 'mdl'), may hold values from -0.09375 to 0.09375
- ref_down: bfloat16 [11008, 4096], P('mdl'), may hold values from -0.109375 to 0.109375
- pol_head: bfloat16 [64000, 4096], P(('grp', 'mdl')), may hold values from -20 to 20
- ref_head: bfloat16 [64000, 4096], P(('grp', 'mdl')), may hold values from -20 to 20
- token_ids: int32 [1024], replicated, may hold values from 0 to 63999
- lengths: int32 [16], replicated, may hold values from 1 to 160, 1024 in all
Outputs:
- pol_out: bfloat16 [1024, 4096], P(('grp', 'mdl'))
- ref_out: bfloat16 [1024, 4096], P(('grp', 'mdl'))
- rollout_ratio: float32 [16], replicated
Inputs may be any that keep to these rules, and one draw needn't show every extreme that they name: Rollout lengths sum to 1024; the longest is exactly 160.
All inputs are finite; a program needn't handle non-finite values.
Results may differ from a plain program's by a relative error of at most 0.012.
The roundings to bfloat16 on the way count: a program that leaves them out, or rounds other values in their place, can miss the bound.
Values may be sent and summed in bfloat16 or wider, within the bound.
No kernel may reach another device: no remote copies, remote signals or barrier semaphores. Data moves between devices by JAX's collectives and lax.ppermute only.
A program may use at most 128 MiB of HBM per device.

v0:
```python
import jax
import jax.numpy as jnp
from jax import lax
from jax.sharding import PartitionSpec as P


def rms_rows(rows, gain):
    values = rows.astype(jnp.float32)
    scale = lax.rsqrt(jnp.mean(values * values, axis=-1, keepdims=True) + 1e-05)
    return (values * scale * gain.astype(jnp.float32)).astype(jnp.bfloat16)


def mlp_partial(piece, gain, w_gate, w_up, w_down):
    normed = rms_rows(piece, gain)
    gate = jnp.dot(normed, w_gate, preferred_element_type=jnp.float32)
    upper = jnp.dot(normed, w_up, preferred_element_type=jnp.float32)
    hidden = (jax.nn.silu(gate) * upper).astype(jnp.bfloat16)
    return jnp.dot(hidden, w_down, preferred_element_type=jnp.float32)


def vocab_terms(token_rows, head_rows, targets, vocab):
    logits = jnp.einsum("td,vd->tv", token_rows, head_rows, preferred_element_type=jnp.float32)
    peak = jnp.max(logits, axis=1)
    total = jnp.sum(jnp.exp(logits - peak[:, None]), axis=1)
    target = jnp.sum(jnp.where(targets[:, None] == vocab[None, :], logits, 0.0), axis=1)
    return (peak, total, target)


def rollout_totals(log_ratio, positions, lengths):
    ends = jnp.cumsum(lengths)
    owner = jnp.sum((positions[:, None] >= ends[None, :]).astype(jnp.int32), axis=1)
    onehot = (owner[:, None] == jnp.arange(lengths.shape[0], dtype=jnp.int32)[None, :]).astype(
        jnp.float32
    )
    return jnp.sum(log_ratio[:, None] * onehot, axis=0)


def per_device(
    pol_hidden,
    ref_hidden,
    pol_mlp_gain,
    ref_mlp_gain,
    pol_final_gain,
    ref_final_gain,
    pol_gate,
    pol_up,
    pol_down,
    ref_gate,
    ref_up,
    ref_down,
    pol_head,
    ref_head,
    token_ids,
    lengths,
):
    rows = pol_hidden.shape[0]
    member = lax.axis_index("mdl")
    group = lax.axis_index("grp")
    members = lax.axis_size("mdl")
    both_in = lax.all_gather(jnp.stack([pol_hidden, ref_hidden]), "mdl", axis=1, tiled=True)
    partials = (
        mlp_partial(both_in[0], pol_mlp_gain, pol_gate, pol_up, pol_down),
        mlp_partial(both_in[1], ref_mlp_gain, ref_gate, ref_up, ref_down),
    )
    mixed = lax.psum(partials, "mdl")
    outs = [(both_in[i].astype(jnp.float32) + mixed[i]).astype(jnp.bfloat16) for i in range(2)]
    finals = jnp.stack([rms_rows(outs[0], pol_final_gain), rms_rows(outs[1], ref_final_gain)])
    own = [lax.dynamic_slice_in_dim(o, member * rows, rows, axis=0) for o in outs]
    every = lax.all_gather(finals, "grp", axis=1, tiled=True)
    voc_dev = pol_head.shape[0]
    positions = jnp.arange(every.shape[1], dtype=jnp.int32)
    vocab = (group * members + member) * voc_dev + jnp.arange(voc_dev, dtype=jnp.int32)
    pol_terms = vocab_terms(every[0], pol_head, token_ids, vocab)
    ref_terms = vocab_terms(every[1], ref_head, token_ids, vocab)
    peaks = lax.pmax(lax.pmax((pol_terms[0], ref_terms[0]), "mdl"), "grp")
    sums = lax.psum(
        lax.psum(
            (
                pol_terms[1] * jnp.exp(pol_terms[0] - peaks[0]),
                pol_terms[2],
                ref_terms[1] * jnp.exp(ref_terms[0] - peaks[1]),
                ref_terms[2],
            ),
            "mdl",
        ),
        "grp",
    )
    pol_logp = sums[1] - peaks[0] - jnp.log(sums[0])
    ref_logp = sums[3] - peaks[1] - jnp.log(sums[2])
    rollout_ratio = rollout_totals(pol_logp - ref_logp, positions, lengths)
    return (own[0], own[1], rollout_ratio)


def solution(mesh):
    placed = (
        P(("grp", "mdl"), None),
        P(("grp", "mdl"), None),
        P(),
        P(),
        P(),
        P(),
        P(None, "mdl"),
        P(None, "mdl"),
        P("mdl", None),
        P(None, "mdl"),
        P(None, "mdl"),
        P("mdl", None),
        P(("grp", "mdl"), None),
        P(("grp", "mdl"), None),
        P(),
        P(),
    )
    return jax.shard_map(
        per_device,
        mesh=mesh,
        in_specs=placed,
        out_specs=(P(("grp", "mdl"), None), P(("grp", "mdl"), None), P()),
        check_vma=False,
    )
```

profile of v0, /device:TPU:8, one launch (start us, length us, event | category | flops | bytes accessed | tf_op | source)
XLA Modules:
  0.0 921.6 jit_solution(18328997950964783200)
XLA Ops:
  7.2 0.0 copy-start
  7.2 0.0 all-gather.3.cloned.1.call-start
  7.2 1.0 pad_maximum_fusion.1
  8.2 0.7 copy.28
  8.9 0.0 all-gather.3.cloned.1.call-update
  8.9 0.0 all-reduce.7.cloned.1.call-start
  9.0 1.3 convert_element_type.62
  10.3 0.7 convert_element_type.68
  11.0 81.7 %all-gather.3.cloned.1.call-done = bf16[2,256,4096]{2,0,1:T(2,128)(2,1)} async-done(((bf16[2,4,4096]{2,0,1:T(2,128)(2,1)}), bf16[2,256,4096]{2,0,1:T(2,128)(2,1)}) %all-gather.3.cloned.1.call-update) | async-done | bytes 4194320 | tf_op jit(solution)/shard_map/all_gather | solution.py:60
  92.7 13.2 %fusion.48 = (bf16[1,256,4096]{2,0,1:T(2,128)(2,1)S(1)}, bf16[1,256,4096]{2,0,1:T(2,128)(2,1)S(1)}) fusion(bf16[2,256,4096]{2,0,1:T(2,128)(2,1)} %all-gather.3.cloned.1.call-done), kind=kLoop, calls=%fused_computation.76 | loop fusion | bytes 8388608 | tf_op jit(solution)/shard_map/slice | solution.py:66
  105.9 0.0 copy-start.8
  105.9 6.7 fusion.8
  112.6 0.6 add_rsqrt_fusion.2
  113.2 0.6 copy-done.2
  113.9 1.6 fusion.30
  115.5 6.6 fusion.21
  122.1 3.7 fusion.26
  125.8 6.6 fusion.20
  132.4 0.0 all-reduce.7.cloned.1.call-update
  132.4 0.2 all-gather.5.cloned.1.call-start
  132.6 0.4 copy-done.9
  133.1 0.0 copy-done.10
  133.1 201.9 %all-reduce.7.cloned.1.call-done = (f32[256,4096]{1,0:T(8,128)}, f32[256,4096]{1,0:T(8,128)}) async-done(((f32[256,4096]{1,0:T(8,128)}, f32[256,4096]{1,0:T(8,128)}), (f32[256,4096]{1,0:T(8,128)}, f32[256,4096]{1,0:T(8,128)})) %all-reduce.7.cloned.1.call-update) | async-done | bytes 8388624 | tf_op jit(solution)/shard_map/psum | solution.py:65
  335.0 3.8 fusion.2
  338.9 0.8 copy-done.5
  339.7 0.8 fusion.5
  340.6 0.6 fusion.16
  341.2 0.7 copy-done.4
  341.9 0.6 fusion.17
  342.5 2.3 pad_maximum_fusion
  344.8 0.0 all-gather.5.cloned.1.call-update
  344.9 0.6 copy-done.13
  345.5 0.1 copy.31
  345.6 0.1 reduce
  345.7 0.1 convert_reduce_fusion
  345.8 1.5 constant_dynamic-slice_fusion.1
  347.3 1.5 constant_dynamic-slice_fusion
  348.8 151.6 %all-gather.5.cloned.1.call-done = bf16[2,1024,4096]{2,1,0:T(8,128)(2,1)} async-done(((bf16[2,256,4096]{2,1,0:T(8,128)(2,1)}), bf16[2,1024,4096]{2,1,0:T(8,128)(2,1)}) %all-gather.5.cloned.1.call-update) | async-done | bytes 16777232 | tf_op jit(solution)/shard_map/all_gather | solution.py:69
  500.4 5.9 fusion.49
  506.3 2.2 copy-done.14
  508.6 0.6 copy-done.15
  509.2 3.4 fusion.50
  512.5 131.0 %all-reduce.2 = (f32[1024]{0:T(1024)S(1)}, f32[1024]{0:T(1024)S(1)}) all-reduce(f32[1024]{0:T(1024)S(1)} %get-tuple-element.35, f32[1024]{0:T(1024)S(1)} %get-tuple-element.33), channel_id=1, replica_groups=mesh['grp'=4,'mdl'=64] {'mdl'}, use_global_device_ids=true, to_apply=%region_21.22 | all-reduce | flops 2048 | bytes 16384 | tf_op jit(solution)/shard_map/pmax | solution.py:75
  643.5 8.4 all-reduce.4
  652.0 1.7 fusion.22
  653.7 246.2 %all-reduce = (f32[1024]{0:T(1024)S(1)}, f32[1024]{0:T(1024)S(1)}, f32[1024]{0:T(1024)S(1)}, f32[1024]{0:T(1024)S(1)}) all-reduce(f32[1024]{0:T(1024)S(1)} %exponential_multiply_fusion, f32[1024]{0:T(1024)S(1)} %get-tuple-element.8, f32[1024]{0:T(1024)S(1)} %exponential_multiply_fusion.1, ...), channel_id=1, replica_groups=mesh['grp'=4,'mdl'=64] {'mdl'}, use_global_device_ids=true, to_apply=%region_24.25 | all-reduce | flops 4096 | bytes 32768 | tf_op jit(solution)/shard_map/psum | solution.py:77
  899.9 14.6 %all-reduce.3 = (f32[1024]{0:T(1024)S(1)}, f32[1024]{0:T(1024)S(1)}, f32[1024]{0:T(1024)S(1)}, f32[1024]{0:T(1024)S(1)}) all-reduce(f32[1024]{0:T(1024)S(1)} %get-tuple-element.9, f32[1024]{0:T(1024)S(1)} %get-tuple-element.10, f32[1024]{0:T(1024)S(1)} %get-tuple-element.11, ...), channel_id=1, replica_groups=mesh['grp'=4,'mdl'=64] {'grp'}, use_global_device_ids=true, to_apply=%region_25.26 | all-reduce | flops 4096 | bytes 32768 | tf_op jit(solution)/shard_map/psum | solution.py:76
  914.5 0.6 select_reduce_fusion
  (34 shorter events, 0.1 us)
Async XLA Ops:
  7.2 493.2 %copy-start = (bf16[250,4096]{1,0:T(8,128)(2,1)S(1)}, bf16[250,4096]{1,0:T(8,128)(2,1)}, u32[]{:S(2)}) copy-start(bf16[250,4096]{1,0:T(8,128)(2,1)} %param.28) | copy-start | bytes 6144004
  7.2 85.5 %all-gather.3.cloned.1.call-start = ((), (), s32[]{:S(2)}) async-start(), calls=%async_computation | async-start | bytes 4259840 | tf_op jit(solution)/shard_map/all_gather | solution.py:60
  8.9 326.1 %all-reduce.7.cloned.1.call-start = ((), (), s32[]{:S(2)}) async-start(), calls=%async_computation.2 | async-start | bytes 16777216 | tf_op jit(solution)/shard_map/psum | solution.py:65
  105.9 8.0 copy-start.8
  105.9 8.0 copy-start.16
  112.6 1.3 copy-start.2
  112.6 1.3 copy-start.12
  113.9 1.6 copy-start.6
  122.1 3.7 copy-start.7
  132.4 0.7 copy-start.9
  132.4 0.7 copy-start.10
  132.4 368.0 %all-gather.5.cloned.1.call-start = ((), (), s32[]{:S(2)}) async-start(), calls=%async_computation.1 | async-start | bytes 20971520 | tf_op jit(solution)/shard_map/all_gather | solution.py:69
  335.0 3.9 copy-start.1
  335.0 4.7 copy-start.5
  338.9 3.0 copy-start.3
  340.6 1.3 copy-start.4
  344.8 0.7 copy-start.13
  500.4 8.2 copy-start.14
  500.4 8.7 copy-start.15
  509.2 142.8 %copy-start.11 = (s32[1024]{0:T(1024)S(1)}, s32[1024]{0:T(1024)}, u32[]{:S(2)}) copy-start(s32[1024]{0:T(1024)} %param.30) | copy-start | bytes 12292
Sparse Core Ops, SparseCore 0:
  10.8 81.8 all-gather.2
  132.5 202.4 all-reduce.6
  345.0 155.3 all-gather.4
where the time goes:
time: 922 us
  waiting for transfers between devices  435 us (47%)
  blocking collectives  400 us (43%)
  matrix products  27.8 us (3%)
  local copies, waits for them, and re-layouts  23 us (2%)
  other arithmetic  21.2 us (2%)
  between operations  13.9 us (2%)
    psum x1, blocking collectives, per_device(): lax.psum((pol_terms[1] * jnp.exp(pol_terms[0] - peaks[0]), pol_terms[2],...  246 us
    psum x1, waiting for transfers between devices, per_device(): mixed = lax.psum(partials, 'mdl')  202 us
    all_gather x1, waiting for transfers between devices, per_device(): every = lax.all_gather(finals, 'grp', axis=1, tiled=True)  152 us
    pmax x2, blocking collectives, per_device(): peaks = lax.pmax(lax.pmax((pol_terms[0], ref_terms[0]), 'mdl'), 'grp')  139 us
    all_gather x1, waiting for transfers between devices, per_device(): lax.all_gather(jnp.stack([pol_hidden, ref_hidden]), 'mdl', axis=1, tiled=...  81.7 us
  transfers between devices with their start and end apart: 3, of which 3 were waited for; matrix products, arithmetic and copies ran while one was open for 1% of the time, Pallas kernels for 0%

commit v1 on v0

--- a/solution.py
+++ b/solution.py
@@ -1,7 +1,29 @@
+import functools
 import jax
 import jax.numpy as jnp
 from jax import lax
 from jax.sharding import PartitionSpec as P
+from jax.lax import axis_index, axis_size, ppermute
+
+
+def _clear_words(u_in, mesh_dim, d_out):
+    n_slots = axis_size(mesh_dim)
+    steps_seen = [(ii, (ii + 1) % n_slots) for ii in range(n_slots)]
+    log = [(ii, (ii - 1) % n_slots) for ii in range(n_slots)]
+    f_now, step_out = ([u_in], [u_in])
+    for _ in range(n_slots // 2):
+        f_now.append(ppermute(f_now[-1], mesh_dim, steps_seen))
+    for _ in tuple(range((n_slots - 1) // 2)):
+        step_out.append(ppermute(step_out[-1], mesh_dim, log))
+    z_new = jnp.roll(
+        jnp.concatenate([*f_now[::-1], *step_out[1:]], axis=d_out),
+        (axis_index(mesh_dim) - n_slots // 2) * u_in.shape[d_out],
+        axis=d_out,
+    )
+    return z_new
+
+
+streams_direct = functools.partial(_clear_words, mesh_dim="grp", d_out=1)
 
 
 def rms_rows(rows, gain):
@@ -66,7 +88,7 @@
     outs = [(both_in[i].astype(jnp.float32) + mixed[i]).astype(jnp.bfloat16) for i in range(2)]
     finals = jnp.stack([rms_rows(outs[0], pol_final_gain), rms_rows(outs[1], ref_final_gain)])
     own = [lax.dynamic_slice_in_dim(o, member * rows, rows, axis=0) for o in outs]
-    every = lax.all_gather(finals, "grp", axis=1, tiled=True)
+    every = streams_direct(finals)
     voc_dev = pol_head.shape[0]
     positions = jnp.arange(every.shape[1], dtype=jnp.int32)
     vocab = (group * members + member) * voc_dev + jnp.arange(voc_dev, dtype=jnp.int32)

time: 922 us -> 985 us (1.068)
  local copies, waits for them, and re-layouts: 23 us -> 48.3 us
  waiting for transfers between devices: 435 us -> 459 us
    ppermute x0 -> x3, waiting for transfers between devices: none -> 175 us  [the longest x2 175 us: _clear_words(): f_now.append(ppermute(f_now[-1], mesh_dim, steps_seen))]
    all_gather x1 -> x0, waiting for transfers between devices: 152 us -> none  [per_device(): every = lax.all_gather(finals, 'grp', axis=1, tiled=True)]
    unnamed x34 -> x45, local copies, waits for them, and re-layouts: 6.11 us -> 26.7 us
  transfers between devices with their start and end apart: 3 -> 5, of which waited for: 3 -> 4; matrix products, arithmetic and copies ran while one was open for 1% -> 2% of each run, Pallas kernels for 0% -> 0%
where the time goes in v1:
time: 985 us; the launch traced here: 984 us
  waiting for transfers between devices  459 us (47%)
  blocking collectives  401 us (41%)
  local copies, waits for them, and re-layouts  48.3 us (5%)
  matrix products  31.1 us (3%)
  other arithmetic  26.4 us (3%)
  between operations  14.3 us (1%)
    psum x1, blocking collectives, per_device(): lax.psum((pol_terms[1] * jnp.exp(pol_terms[0] - peaks[0]), pol_terms[2],...  246 us
    psum x1, waiting for transfers between devices, per_device(): mixed = lax.psum(partials, 'mdl')  202 us
    ppermute x2, waiting for transfers between devices, _clear_words(): f_now.append(ppermute(f_now[-1], mesh_dim, steps_seen))  175 us
    pmax x2, blocking collectives, per_device(): peaks = lax.pmax(lax.pmax((pol_terms[0], ref_terms[0]), 'mdl'), 'grp')  142 us
    all_gather x1, waiting for transfers between devices, per_device(): lax.all_gather(jnp.stack([pol_hidden, ref_hidden]), 'mdl', axis=1, tiled=...  81.7 us
    unnamed x45, local copies, waits for them, and re-layouts  26.7 us
  transfers between devices with their start and end apart: 5, of which 4 were waited for; matrix products, arithmetic and copies ran while one was open for 2% of the time, Pallas kernels for 0%

profile of v1, /device:TPU:8, one launch (start us, length us, event | category | flops | bytes accessed | tf_op | source)
XLA Modules:
  0.0 983.7 jit_solution(6969346762227151689)
XLA Ops:
  7.2 1.0 pad_maximum_fusion.1
  8.2 0.7 copy.28
  9.0 1.3 convert_element_type.62
  10.3 0.7 convert_element_type.68
  11.0 81.7 %all-gather.2.cloned.1.call-done = bf16[2,256,4096]{2,0,1:T(2,128)(2,1)} async-done(((bf16[2,4,4096]{2,0,1:T(2,128)(2,1)}), bf16[2,256,4096]{2,0,1:T(2,128)(2,1)}) %all-gather.2.cloned.1.call-update) | async-done | bytes 4194320 | tf_op jit(solution)/shard_map/all_gather | solution.py:82
  92.7 13.2 %fusion.50 = (bf16[1,256,4096]{2,0,1:T(2,128)(2,1)S(1)}, bf16[1,256,4096]{2,0,1:T(2,128)(2,1)S(1)}) fusion(bf16[2,256,4096]{2,0,1:T(2,128)(2,1)} %all-gather.2.cloned.1.call-done), kind=kLoop, calls=%fused_computation.86 | loop fusion | bytes 8388608 | tf_op jit(solution)/shard_map/slice | solution.py:88
  105.9 6.7 fusion.8
  112.6 0.6 add_rsqrt_fusion.2
  113.2 0.7 copy-done.6
  113.9 1.6 fusion.30
  115.5 6.6 fusion.21
  122.1 3.7 fusion.26
  125.8 6.6 fusion.20
  132.4 0.7 copy-done.13
  133.1 202.1 %all-reduce.7.cloned.1.call-done = (f32[256,4096]{1,0:T(8,128)}, f32[256,4096]{1,0:T(8,128)}) async-done(((f32[256,4096]{1,0:T(8,128)}, f32[256,4096]{1,0:T(8,128)}), (f32[256,4096]{1,0:T(8,128)}, f32[256,4096]{1,0:T(8,128)})) %all-reduce.7.cloned.1.call-update) | async-done | bytes 8388624 | tf_op jit(solution)/shard_map/psum | solution.py:87
  335.2 4.0 fusion.2
  339.3 0.7 copy-done.9
  339.9 0.9 fusion.5
  340.9 0.6 fusion.16
  341.5 0.6 copy-done.8
  342.1 0.6 fusion.17
  342.8 2.6 pad_maximum_fusion
  345.4 1.5 collective-permute-start
  346.9 89.7 %collective-permute-done = bf16[2,256,4096]{2,1,0:T(8,128)(2,1)} collective-permute-done((bf16[2,256,4096]{2,1,0:T(8,128)(2,1)}, bf16[2,256,4096]{2,1,0:T(8,128)(2,1)}, u32[]{:S(2)}, u32[]{:S(2)}) %collective-permute-start) | collective-permute-done | bytes 4194336 | tf_op jit(solution)/shard_map/ppermute | solution.py:15
  436.6 1.5 collective-permute-start.1
  438.1 0.5 collective-permute-start.2
  438.6 0.1 copy.31
  438.7 0.1 reduce
  438.9 0.1 convert_reduce_fusion
  439.0 1.5 constant_dynamic-slice_fusion.1
  440.4 1.5 constant_dynamic-slice_fusion
  441.9 85.0 %collective-permute-done.1 = bf16[2,256,4096]{2,1,0:T(8,128)(2,1)} collective-permute-done((bf16[2,256,4096]{2,1,0:T(8,128)(2,1)}, bf16[2,256,4096]{2,1,0:T(8,128)(2,1)}, u32[]{:S(2)}, u32[]{:S(2)}) %collective-permute-start.1) | collective-permute-done | bytes 4194336 | tf_op jit(solution)/shard_map/ppermute | solution.py:15
  526.9 4.8 constant_dynamic-update-slice_fusion.7
  531.7 4.8 constant_dynamic-update-slice_fusion.6
  536.5 2.4 constant_dynamic-update-slice_fusion.5
  538.9 4.8 constant_dynamic-update-slice_fusion.4
  543.6 4.9 constant_dynamic-update-slice_fusion.3
  548.5 4.7 constant_dynamic-update-slice_fusion.2
  553.2 2.4 constant_dynamic-update-slice_fusion.1
  555.6 4.7 constant_dynamic-update-slice_fusion
  560.3 5.9 fusion.51
  566.2 6.7 fusion.52
  573.0 131.3 %all-reduce.2 = (f32[1024]{0:T(1024)S(1)}, f32[1024]{0:T(1024)S(1)}) all-reduce(f32[1024]{0:T(1024)S(1)} %get-tuple-element.35, f32[1024]{0:T(1024)S(1)} %get-tuple-element.33), channel_id=1, replica_groups=mesh['grp'=4,'mdl'=64] {'mdl'}, use_global_device_ids=true, to_apply=%region_21.22 | all-reduce | flops 2048 | bytes 16384 | tf_op jit(solution)/shard_map/pmax | solution.py:97
  704.3 10.5 %all-reduce.4 = (f32[1024]{0:T(1024)S(1)}, f32[1024]{0:T(1024)S(1)}) all-reduce(f32[1024]{0:T(1024)S(1)} %get-tuple-element.15, f32[1024]{0:T(1024)S(1)} %get-tuple-element.16), channel_id=1, replica_groups=mesh['grp'=4,'mdl'=64] {'grp'}, use_global_device_ids=true, to_apply=%region_22.23 | all-reduce | flops 2048 | bytes 16384 | tf_op jit(solution)/shard_map/pmax | solution.py:97
  714.8 1.7 fusion.22
  716.5 246.2 %all-reduce = (f32[1024]{0:T(1024)S(1)}, f32[1024]{0:T(1024)S(1)}, f32[1024]{0:T(1024)S(1)}, f32[1024]{0:T(1024)S(1)}) all-reduce(f32[1024]{0:T(1024)S(1)} %exponential_multiply_fusion, f32[1024]{0:T(1024)S(1)} %get-tuple-element.8, f32[1024]{0:T(1024)S(1)} %exponential_multiply_fusion.1, ...), channel_id=1, replica_groups=mesh['grp'=4,'mdl'=64] {'mdl'}, use_global_device_ids=true, to_apply=%region_24.25 | all-reduce | flops 4096 | bytes 32768 | tf_op jit(solution)/shard_map/psum | solution.py:99
  962.7 13.5 %all-reduce.3 = (f32[1024]{0:T(1024)S(1)}, f32[1024]{0:T(1024)S(1)}, f32[1024]{0:T(1024)S(1)}, f32[1024]{0:T(1024)S(1)}) all-reduce(f32[1024]{0:T(1024)S(1)} %get-tuple-element.9, f32[1024]{0:T(1024)S(1)} %get-tuple-element.10, f32[1024]{0:T(1024)S(1)} %get-tuple-element.11, ...), channel_id=1, replica_groups=mesh['grp'=4,'mdl'=64] {'grp'}, use_global_device_ids=true, to_apply=%region_25.26 | all-reduce | flops 4096 | bytes 32768 | tf_op jit(solution)/shard_map/psum | solution.py:98
  976.2 0.6 select_reduce_fusion
  (51 shorter events, 0.3 us)
Async XLA Ops:
  7.2 553.1 %copy-start = (bf16[250,4096]{1,0:T(8,128)(2,1)S(1)}, bf16[250,4096]{1,0:T(8,128)(2,1)}, u32[]{:S(2)}) copy-start(bf16[250,4096]{1,0:T(8,128)(2,1)} %param.28) | copy-start | bytes 6144004
  7.2 85.5 %all-gather.2.cloned.1.call-start = ((), (), s32[]{:S(2)}) async-start(), calls=%async_computation | async-start | bytes 4259840 | tf_op jit(solution)/shard_map/all_gather | solution.py:82
  8.9 326.3 %all-reduce.7.cloned.1.call-start = ((), (), s32[]{:S(2)}) async-start(), calls=%async_computation.1 | async-start | bytes 16777216 | tf_op jit(solution)/shard_map/psum | solution.py:87
  105.9 8.0 copy-start.12
  105.9 8.0 copy-start.19
  112.6 1.3 copy-start.6
  112.6 2.9 copy-start.10
  112.6 1.3 copy-start.16
  122.1 3.7 copy-start.11
  132.4 0.7 copy-start.13
  132.4 0.7 copy-start.14
  335.2 4.0 copy-start.5
  335.2 4.7 copy-start.9
  339.2 2.9 copy-start.7
  340.8 1.3 copy-start.8
  342.1 3.2 copy-start.1
  342.8 2.6 copy-start.3
  342.8 95.8 %copy-start.17 = (s32[16]{0:T(128)S(1)}, s32[16]{0:T(128)}, u32[]{:S(2)}) copy-start(s32[16]{0:T(128)} %param.31) | copy-start | bytes 196
  345.4 91.2 %collective-permute-start = (bf16[2,256,4096]{2,1,0:T(8,128)(2,1)}, bf16[2,256,4096]{2,1,0:T(8,128)(2,1)}, u32[]{:S(2)}, u32[]{:S(2)}) collective-permute-start(bf16[2,256,4096]{2,1,0:T(8,128)(2,1)} %pad_maximum_fusion), channel_id=1, source_target_pairs={{0,64},{64,128},{128,192},{192,0},{1,65},{65,129},{129,193},{193,1... | collective-permute-start | bytes 12582920 | tf_op jit(solution)/shard_map/ppermute | solution.py:15
  436.6 90.3 %collective-permute-start.1 = (bf16[2,256,4096]{2,1,0:T(8,128)(2,1)}, bf16[2,256,4096]{2,1,0:T(8,128)(2,1)}, u32[]{:S(2)}, u32[]{:S(2)}) collective-permute-start(bf16[2,256,4096]{2,1,0:T(8,128)(2,1)} %collective-permute-done), channel_id=1, source_target_pairs={{0,64},{64,128},{128,192},{192,0},{1,65},{65,129},{129,193},{193,1... | collective-permute-start | bytes 12582920 | tf_op jit(solution)/shard_map/ppermute | solution.py:15
  438.1 100.8 %collective-permute-start.2 = (bf16[2,256,4096]{2,1,0:T(8,128)(2,1)}, bf16[2,256,4096]{2,1,0:T(8,128)(2,1)}, u32[]{:S(2)}, u32[]{:S(2)}) collective-permute-start(bf16[2,256,4096]{2,1,0:T(8,128)(2,1)} %pad_maximum_fusion), channel_id=1, source_target_pairs={{0,192},{64,0},{128,64},{192,128},{1,193},{65,1},{129,65},{193,129... | collective-permute-start | bytes 12582920 | tf_op jit(solution)/shard_map/ppermute | solution.py:17
  531.7 4.8 copy-start.2
  531.7 4.8 copy-start.4
  560.3 5.9 copy-start.18
  566.2 148.5 %copy-start.15 = (s32[1024]{0:T(1024)S(1)}, s32[1024]{0:T(1024)}, u32[]{:S(2)}) copy-start(s32[1024]{0:T(1024)} %param.30) | copy-start | bytes 12292
Sparse Core Ops, SparseCore 0:
  10.8 81.8 all-gather.1
  132.5 202.6 all-reduce.6
